TPU v7x, 256 devices: a whole 4x4x8 slice. The times are simulated.
256 devices in a mesh: dp: 32 (over y, z), fsdp: 8 (over x, core).
Axes of the slice: x: 4, y: 4, z: 8, core: 2. Of those that a mesh axis runs over, the one named last changes fastest.
Arguments:
- prefill_tokens: bfloat16 [16384, 2048], P('dp'), may hold values from -3 to 3
- decode_tokens: bfloat16 [128, 2048], P('dp'), may hold values from -3 to 3
- query_weight: bfloat16 [2048, 2048], P('dp', 'fsdp'), may hold values from -0.125 to 0.125
- key_weight: bfloat16 [2048, 2048], P('dp', 'fsdp'), may hold values from -0.125 to 0.125
- value_weight: bfloat16 [2048, 2048], P('dp', 'fsdp'), may hold values from -0.125 to 0.125
- out_weight: bfloat16 [2048, 2048], P('fsdp', 'dp'), may hold values from -0.125 to 0.125
- prior_keys: bfloat16 [32, 2048, 2048], P('dp', None, 'fsdp'), may hold values from -480 to 480
- prior_values: bfloat16 [32, 2048, 2048], P('dp', None, 'fsdp'), may hold values from -6 to 6
- prior_length: int32 [32], P('dp'), may hold values from 0 to 2048, as said below
- pool_keys: bfloat16 [1536, 128, 2048], P('dp', None, 'fsdp'), may hold values from -480 to 480
- pool_values: bfloat16 [1536, 128, 2048], P('dp', None, 'fsdp'), may hold values from -6 to 6
- page_slots: int32 [1536], replicated, may hold values from 0 to 1535, each once
- page_counts: int32 [128], replicated, may hold values from 1 to 128, 1536 in all
- last_fill: int32 [128], replicated, may hold values from 1 to 128
- decode_request: int32 [128], replicated, may hold values from 0 to 127, each once
Outputs:
- mixed_prefill: bfloat16 [16384, 2048], P('dp', 'fsdp')
- mixed_decode: bfloat16 [128, 2048], P('dp', 'fsdp')
Inputs may be any that keep to these rules, and one draw needn't show every extreme that they name: `prior_length`: one prefill request's prior fills all 2048 slots. Request r owns the logical pages first_page[r] to first_page[r] + page_counts[r] - 1; the counts sum to 1536, and some request has exactly 128 pages. A permutation: pool slot page_slots[k] holds logical page k. `decode_request`: A permutation of the decode requests.
All inputs are finite; a program needn't handle non-finite values.
Results may differ from a plain program's by a relative error of at most 0.015.
The roundings to bfloat16 on the way count: a program that leaves them out, or rounds other values in their place, can miss the bound.
Values may be sent and summed in bfloat16 or wider, within the bound.
No kernel may reach another device: no remote copies, remote signals or barrier semaphores. Data moves between devices by JAX's collectives and lax.ppermute only.
A program may use at most 128 MiB of HBM per device.

v0:
```python
import jax
import jax.numpy as jnp
from jax import lax
from jax.sharding import PartitionSpec as P

HEAD = 128
PAGE = 128
EPSILON = 1e-05
ROPE_BASE = 10000.0
NEG_FILL = -1e30


def merged(value, axis, join):
    pieces = jax.tree.map(lambda part: lax.all_gather(part, axis), value)
    head = jax.tree.map(lambda part: part[0], pieces)
    tail = jax.tree.map(lambda part: part[1:], pieces)
    total, _ = lax.scan(lambda total, share: (join(total, share), None), head, tail)
    return total


def layer_norm(rows_in):
    widened = rows_in.astype(jnp.float32)
    average = jnp.mean(widened, axis=-1, keepdims=True)
    centred = widened - average
    variance = jnp.mean(centred * centred, axis=-1, keepdims=True)
    return (centred * lax.rsqrt(variance + EPSILON)).astype(jnp.bfloat16)


def rotary(vectors, positions, head_size):
    row_count = vectors.shape[0]
    split_heads = vectors.reshape(row_count, -1, head_size)
    halfway = head_size // 2
    exponent = jnp.arange(halfway, dtype=jnp.float32) * (2.0 / head_size)
    frequency = jnp.power(jnp.float32(ROPE_BASE), -exponent)
    angles = positions.astype(jnp.float32)[:, None] * frequency[None, :]
    cosine = jnp.cos(angles)[:, None, :]
    sine_part = jnp.sin(angles)[:, None, :]
    leading = split_heads[..., :halfway]
    trailing = split_heads[..., halfway:]
    turned = jnp.concatenate(
        [leading * cosine - trailing * sine_part, trailing * cosine + leading * sine_part], axis=-1
    )
    return turned.reshape(row_count, -1)


def rescale(vectors, factor, head_size):
    shaped = vectors.reshape(vectors.shape[0], factor.shape[1], head_size)
    return (shaped * factor[:, :, None]).reshape(vectors.shape)


def combine_pair(earlier, later):
    early_top, early_total, early_mix = earlier
    late_top, late_total, late_mix = later
    joined_top = jnp.maximum(early_top, late_top)
    early_factor = jnp.exp(early_top - joined_top)
    late_factor = jnp.exp(late_top - joined_top)
    joined_total = early_total * early_factor + late_total * late_factor
    joined_mix = rescale(early_mix, early_factor, HEAD) + rescale(late_mix, late_factor, HEAD)
    return (joined_top, joined_total, joined_mix)


def per_device(
    prefill_tokens,
    decode_tokens,
    query_weight,
    key_weight,
    value_weight,
    out_weight,
    prior_keys,
    prior_values,
    prior_length,
    pool_keys,
    pool_values,
    page_slots,
    page_counts,
    last_fill,
    decode_request,
):
    group_rows = prefill_tokens.shape[0]
    decode_rows = decode_tokens.shape[0]
    local_width = query_weight.shape[1]
    head_count = local_width // HEAD
    score_scale = HEAD ** (-0.5)
    data_index = lax.axis_index("dp")
    model_index = lax.axis_index("fsdp")
    tokens = jnp.concatenate([prefill_tokens, decode_tokens], axis=0)
    normed = layer_norm(tokens)
    portions = (
        lax.all_gather(query_weight, "dp", axis=0, tiled=True),
        lax.all_gather(key_weight, "dp", axis=0, tiled=True),
        lax.all_gather(value_weight, "dp", axis=0, tiled=True),
    )
    raw_queries, raw_keys, raw_values = tuple(
        (jnp.dot(normed, portion, preferred_element_type=jnp.float32) for portion in portions)
    )
    cache_length = (page_counts - 1) * PAGE + last_fill
    first_page = jnp.cumsum(page_counts) - page_counts
    request_count = decode_request.shape[0]
    slot_numbers = jnp.arange(request_count, dtype=jnp.int32)
    slot_of_request = jnp.zeros((request_count,), jnp.int32).at[decode_request].set(slot_numbers)
    my_slots = data_index * decode_rows + jnp.arange(decode_rows, dtype=jnp.int32)
    my_requests = jnp.take(decode_request, my_slots)
    positions = jnp.concatenate(
        [
            prior_length[0] + jnp.arange(group_rows, dtype=jnp.int32),
            jnp.take(cache_length, my_requests),
        ]
    )
    queries = rotary(raw_queries, positions, HEAD).astype(jnp.bfloat16)
    keys_new = rotary(raw_keys, positions, HEAD).astype(jnp.bfloat16)
    values_new = raw_values.astype(jnp.bfloat16)
    prior_slots = prior_keys.shape[1]
    group_queries = queries[:group_rows].reshape(group_rows, head_count, HEAD)
    group_keys = keys_new[:group_rows].reshape(group_rows, head_count, HEAD)
    group_values = values_new[:group_rows].reshape(group_rows, head_count, HEAD)
    stored_keys = prior_keys[0].reshape(prior_slots, head_count, HEAD)
    stored_values = prior_values[0].reshape(prior_slots, head_count, HEAD)
    prior_scores = (
        jnp.einsum("qhd,khd->hqk", group_queries, stored_keys, preferred_element_type=jnp.float32)
        * score_scale
    )
    prior_live = jnp.arange(prior_slots, dtype=jnp.int32) < prior_length[0]
    prior_scores = jnp.where(prior_live[None, None, :], prior_scores, NEG_FILL)
    group_scores = (
        jnp.einsum("qhd,khd->hqk", group_queries, group_keys, preferred_element_type=jnp.float32)
        * score_scale
    )
    causal = jnp.arange(group_rows)[None, :] <= jnp.arange(group_rows)[:, None]
    group_scores = jnp.where(causal[None], group_scores, NEG_FILL)
    row_top = jnp.maximum(
        jnp.max(prior_scores, axis=2, keepdims=True), jnp.max(group_scores, axis=2, keepdims=True)
    )
    prior_weights = jnp.exp(prior_scores - row_top)
    group_weights = jnp.exp(group_scores - row_top)
    weight_total = jnp.sum(prior_weights, axis=2) + jnp.sum(group_weights, axis=2)
    combined = jnp.einsum(
        "hqk,khd->qhd",
        prior_weights.astype(jnp.bfloat16),
        stored_values,
        preferred_element_type=jnp.float32,
    )
    combined = combined + jnp.einsum(
        "hqk,khd->qhd",
        group_weights.astype(jnp.bfloat16),
        group_values,
        preferred_element_type=jnp.float32,
    )
    prefill_attended = (
        (combined / jnp.transpose(weight_total)[:, :, None])
        .reshape(group_rows, local_width)
        .astype(jnp.bfloat16)
    )
    own_queries = queries[group_rows:]
    slot_queries = lax.all_gather(own_queries, "dp", axis=0, tiled=True)
    pool_count = page_slots.shape[0]
    pool_local = pool_keys.shape[0]
    logical_of_slot = (
        jnp.zeros((pool_count,), jnp.int32)
        .at[page_slots]
        .set(jnp.arange(pool_count, dtype=jnp.int32))
    )
    local_logical = lax.dynamic_slice_in_dim(logical_of_slot, data_index * pool_local, pool_local)
    page_owner = (
        jnp.sum((first_page[None, :] <= local_logical[:, None]).astype(jnp.int32), axis=1) - 1
    )
    page_number = local_logical - jnp.take(first_page, page_owner)
    page_slot = jnp.take(slot_of_request, page_owner)
    page_queries = jnp.take(slot_queries, page_slot, axis=0).reshape(pool_local, head_count, HEAD)
    page_keys = pool_keys.reshape(pool_local, PAGE, head_count, HEAD)
    page_scores = (
        jnp.einsum("phd,pkhd->phk", page_queries, page_keys, preferred_element_type=jnp.float32)
        * score_scale
    )
    key_place = page_number[:, None] * PAGE + jnp.arange(PAGE, dtype=jnp.int32)[None, :]
    page_live = key_place < jnp.take(cache_length, page_owner)[:, None]
    page_scores = jnp.where(page_live[:, None, :], page_scores, NEG_FILL)
    member = page_slot[:, None] == slot_numbers[None, :]
    page_top = jnp.max(page_scores, axis=2)
    slot_top = jnp.max(jnp.where(member[:, :, None], page_top[:, None, :], NEG_FILL), axis=0)
    page_weights = jnp.exp(page_scores - jnp.take(slot_top, page_slot, axis=0)[:, :, None])
    member_weights = member.astype(jnp.float32)
    slot_total = jnp.dot(
        member_weights.T, jnp.sum(page_weights, axis=2), precision=lax.Precision.HIGHEST
    )
    page_values = pool_values.reshape(pool_local, PAGE, head_count, HEAD).astype(jnp.float32)
    page_mix = jnp.einsum(
        "phk,pkhd->phd", page_weights, page_values, precision=lax.Precision.HIGHEST
    )
    slot_mix = jnp.dot(
        member_weights.T, page_mix.reshape(pool_local, local_width), precision=lax.Precision.HIGHEST
    )
    merged_top, merged_total, merged_mix = merged(
        (slot_top, slot_total, slot_mix), "dp", combine_pair
    )
    mine_top = lax.dynamic_slice_in_dim(merged_top, data_index * decode_rows, decode_rows, 0)
    mine_total = lax.dynamic_slice_in_dim(merged_total, data_index * decode_rows, decode_rows, 0)
    mine_mix = lax.dynamic_slice_in_dim(merged_mix, data_index * decode_rows, decode_rows, 0)
    own_keys = keys_new[group_rows:].reshape(decode_rows, head_count, HEAD)
    own_score = (
        jnp.einsum(
            "rhd,rhd->rh",
            own_queries.reshape(decode_rows, head_count, HEAD),
            own_keys,
            preferred_element_type=jnp.float32,
        )
        * score_scale
    )
    final_top = jnp.maximum(mine_top, own_score)
    cache_factor = jnp.exp(mine_top - final_top)
    own_factor = jnp.exp(own_score - final_top)
    final_total = mine_total * cache_factor + own_factor
    final_mix = rescale(mine_mix, cache_factor, HEAD) + rescale(
        values_new[group_rows:].astype(jnp.float32), own_factor, HEAD
    )
    decode_attended = rescale(final_mix, 1.0 / final_total, HEAD).astype(jnp.bfloat16)
    attended = jnp.concatenate([prefill_attended, decode_attended], axis=0)
    residual = lax.dynamic_slice_in_dim(tokens, model_index * local_width, local_width, 1)
    terms = jnp.dot(
        attended,
        lax.all_gather(out_weight, "dp", axis=1, tiled=True),
        preferred_element_type=jnp.float32,
    )
    branch = lax.psum_scatter(
        terms.astype(jnp.bfloat16), "fsdp", scatter_dimension=1, tiled=True
    ).astype(jnp.float32)
    result = (residual.astype(jnp.float32) + branch).astype(jnp.bfloat16)
    return (result[:group_rows], result[group_rows:])


def solution(mesh):
    in_specs = (
        P("dp", None),
        P("dp", None),
        P("dp", "fsdp"),
        P("dp", "fsdp"),
        P("dp", "fsdp"),
        P("fsdp", "dp"),
        P("dp", None, "fsdp"),
        P("dp", None, "fsdp"),
        P("dp"),
        P("dp", None, "fsdp"),
        P("dp", None, "fsdp"),
        P(),
        P(),
        P(),
        P(),
    )
    out_specs = (P("dp", "fsdp"), P("dp", "fsdp"))
    return jax.shard_map(
        per_device, mesh=mesh, in_specs=in_specs, out_specs=out_specs, check_vma=False
    )
```

profile of v0, /device:TPU:8, one launch (start us, length us, event | category | flops | bytes accessed | tf_op | source)
XLA Modules:
  0.0 472.7 jit_solution(2688506723281561803)
XLA Ops:
  11.9 6.2 %scatter_custom_fusion.1 = s32[1536]{0:T(1024)S(1)} fusion(s32[1536]{0:T(1024)S(1)} %compare_select_fusion, s32[1536]{0:T(1024)S(1)} %iota.55, s32[]{:T(128)} %constant.45.clone.1), kind=kCustom, calls=%fused_computation.111 | custom fusion | bytes 6148 | tf_op jit(solution)/shard_map/scatter | solution.py:160
  24.2 4.7 %copy.120 = bf16[48,128,256]{1,2,0:T(8,128)(2,1)} copy(bf16[48,128,256]{2,1,0:T(8,128)(2,1)} %param.30) | data formatting | bytes 6291456 | tf_op jit(solution)/shard_map/reshape | solution.py:169
  28.9 1.7 constant_dynamic-update-slice_fusion.1
  31.8 1.9 fusion.9
  35.9 1.8 multiply_cosine_fusion
  37.9 50.8 %all-gather.10.cloned.1.call-done = bf16[2048,256]{1,0:T(8,128)(2,1)} async-done(((bf16[64,256]{1,0:T(8,128)(2,1)}), bf16[2048,256]{1,0:T(8,128)(2,1)}) %all-gather.10.cloned.1.call-update) | async-done | bytes 1048592 | tf_op jit(solution)/shard_map/all_gather | solution.py:89
  88.7 3.4 fusion.77
  92.1 2.1 reshape.284
  94.2 71.0 %all-gather.12.cloned.1.call-done = bf16[2048,256]{1,0:T(8,128)(2,1)} async-done(((bf16[64,256]{1,0:T(8,128)(2,1)}), bf16[2048,256]{1,0:T(8,128)(2,1)}) %all-gather.12.cloned.1.call-update) | async-done | bytes 1048592 | tf_op jit(solution)/shard_map/all_gather | solution.py:90
  165.2 3.4 fusion.78
  168.6 2.1 reshape.285
  170.7 2.7 fusion.74
  175.2 47.6 %all-gather.3 = bf16[32,4,256]{2,1,0:T(4,128)(2,1)S(1)} all-gather(bf16[1,4,256]{2,1,0:T(4,128)(2,1)S(1)} %bitcast.127), channel_id=1, replica_groups=mesh['dp'=32,'fsdp'=8] {'dp'}, dimensions={0}, use_global_device_ids=true | all-gather | bytes 67584 | tf_op jit(solution)/shard_map/all_gather | solution.py:154
  224.3 2.8 fusion.44
  230.5 2.5 fusion.13
  233.0 1.7 fusion.39
  236.2 2.3 copy.118
  238.4 2.2 reshape_squeeze.6
  240.6 41.6 %all-gather = f32[4096,2]{0,1:T(2,128)S(1)} all-gather(f32[128,2]{0,1:T(2,128)S(1)} %select_reduce_fusion), channel_id=2, replica_groups=mesh['dp'=32,'fsdp'=8] {'dp'}, dimensions={0}, use_global_device_ids=true | all-gather | bytes 33792 | tf_op jit(solution)/shard_map/all_gather | solution.py:14
  283.0 41.3 %all-gather.1 = f32[4096,2]{0,1:T(2,128)S(1)} all-gather(f32[128,2]{0,1:T(2,128)S(1)} %fusion.50), channel_id=3, replica_groups=mesh['dp'=32,'fsdp'=8] {'dp'}, dimensions={0}, use_global_device_ids=true | all-gather | bytes 33792 | tf_op jit(solution)/shard_map/all_gather | solution.py:14
  324.9 3.3 fusion.16
  328.3 1.6 fusion.3
  329.9 1.9 fusion.4
  331.8 2.8 fusion.19
  334.6 2.6 convolution_convert_fusion.1
  338.7 1.8 copy.119
  340.5 2.1 fusion.17
  342.6 3.2 fusion.24
  345.8 4.5 slice.113
  350.3 72.1 %while.14 = (s32[]{:T(128)}, f32[128,2]{0,1:T(2,128)S(1)}, f32[128,2]{0,1:T(2,128)S(1)}, f32[128,256]{1,0:T(8,128)S(1)}, f32[31,128,2]{1,2,0:T(2,128)}, /*index=...) while((s32[]{:T(128)}, f32[128,2]{0,1:T(2,128)S(1)}, f32[128,2]{0,1:T(2,128)S(1)}, ...), condition=%wide.region_14.17_spmd, body=%wide.region_13.16_spmd.sunk | while | flops 99842 | bytes 931941 | solution.py:17
  423.8 3.7 convolution_convert_fusion
  427.5 36.0 %reduce-scatter.2.cloned.1.call-done = bf16[516,256]{1,0:T(8,128)(2,1)} async-done(((bf16[516,2048]{1,0:T(8,128)(2,1)}), bf16[516,256]{1,0:T(8,128)(2,1)}) %reduce-scatter.2.cloned.1.call-update) | async-done | bytes 264208 | tf_op jit(solution)/shard_map/reduce_scatter | solution.py:223
  (316 shorter events, 99.7 us)
Async XLA Ops:
  7.2 223.3 %copy-start = (bf16[48,128,256]{2,1,0:T(8,128)(2,1)S(1)}, bf16[48,128,256]{2,1,0:T(8,128)(2,1)}, u32[]{:S(2)}) copy-start(bf16[48,128,256]{2,1,0:T(8,128)(2,1)} %param.31) | copy-start | bytes 9437188
  7.2 81.5 %all-gather.10.cloned.1.call-start = ((), (), s32[]{:S(2)}) async-start(), calls=%async_computation.1 | async-start | bytes 1081344 | tf_op jit(solution)/shard_map/all_gather | solution.py:89
  7.9 157.3 %all-gather.12.cloned.1.call-start = ((), (), s32[]{:S(2)}) async-start(), calls=%async_computation.2 | async-start | bytes 1081344 | tf_op jit(solution)/shard_map/all_gather | solution.py:90
  8.7 326.0 %all-gather.14.cloned.1.call-start = ((), (), s32[]{:S(2)}) async-start(), calls=%async_computation.3 | async-start | bytes 1081344 | tf_op jit(solution)/shard_map/all_gather | solution.py:91
  9.4 336.4 %all-gather.18.cloned.1.call-start = ((), (), s32[]{:S(2)}) async-start(), calls=%async_computation.6 | async-start | bytes 4325376 | tf_op jit(solution)/shard_map/all_gather | solution.py:14
  23.5 5.4 %copy-start.17 = (s32[48]{0:T(128)}, s32[48]{0:T(128)S(1)}, u32[]{:S(2)}) copy-start(s32[48]{0:T(128)S(1)} %get-tuple-element.103) | copy-start | bytes 580
  28.9 1.7 copy-start.15
  30.7 3.0 copy-start.1
  35.8 186.9 %copy-start.16 = (s32[1024]{0:T(1024)}, s32[1024]{0:T(1024)S(1)}, u32[]{:S(2)}) copy-start(s32[1024]{0:T(1024)S(1)} %pad_clamp_fusion) | copy-start | bytes 12292
  37.9 189.2 %copy-start.14 = (pred[48,128]{1,0:T(8,128)(4,1)}, pred[48,128]{1,0:T(8,128)(4,1)S(1)}, u32[]{:S(2)}) copy-start(pred[48,128]{1,0:T(8,128)(4,1)S(1)} %add_compare_fusion) | copy-start | bytes 18436
  170.7 2.7 copy-start.7
  170.7 2.7 copy-start.8
  173.7 0.7 copy-start.3
  173.7 1.4 copy-start.5
  173.7 1.4 copy-start.6
  233.0 49.8 %copy-start.18 = (s32[48]{0:T(128)S(1)}, s32[48]{0:T(128)}, u32[]{:S(2)}) copy-start(s32[48]{0:T(128)} %copy-done.17) | copy-start | bytes 580
  234.7 189.1 %all-gather.16.cloned.1.call-start = ((), (), s32[]{:S(2)}) async-start(), calls=%async_computation.4 | async-start | bytes 1081344 | tf_op jit(solution)/shard_map/all_gather | solution.py:220
  235.3 228.2 %reduce-scatter.2.cloned.1.call-start = ((), (), s32[]{:S(2)}) async-start(), calls=%async_computation.5 | async-start | bytes 2396160 | tf_op jit(solution)/shard_map/reduce_scatter | solution.py:223
  240.6 87.7 %copy-start.2 = (bf16[2048,2,128]{2,1,0:T(2,128)(2,1)S(1)}, bf16[2048,2,128]{2,1,0:T(2,128)(2,1)}, u32[]{:S(2)}) copy-start(bf16[2048,2,128]{2,1,0:T(2,128)(2,1)} %reshape_squeeze.6) | copy-start | bytes 3145732
  240.6 87.7 %copy-start.4 = (bf16[516,2,64]{2,0,1:T(8,128)(2,1)S(1)}, bf16[516,2,64]{2,0,1:T(8,128)(2,1)}, u32[]{:S(2)}) copy-start(bf16[516,2,64]{2,0,1:T(8,128)(2,1)} %copy-done.3) | copy-start | bytes 396292
  282.2 47.7 %copy-start.12 = (f32[4096,2]{0,1:T(2,128)}, f32[4096,2]{0,1:T(2,128)S(1)}, u32[]{:S(2)}) copy-start(f32[4096,2]{0,1:T(2,128)S(1)} %all-gather) | copy-start | bytes 98308
  324.3 5.6 %copy-start.13 = (f32[4096,2]{0,1:T(2,128)}, f32[4096,2]{0,1:T(2,128)S(1)}, u32[]{:S(2)}) copy-start(f32[4096,2]{0,1:T(2,128)S(1)} %all-gather.1) | copy-start | bytes 98308
  329.9 1.9 copy-start.10
  334.6 5.9 %copy-start.9 = (pred[512,512]{0,1:T(8,128)(4,1)S(1)}, pred[512,512]{0,1:T(8,128)(4,1)}, u32[]{:S(2)}) copy-start(pred[512,512]{0,1:T(8,128)(4,1)} %iota_compare_fusion) | copy-start | bytes 786436
  337.3 0.7 copy-start.11
  345.8 4.5 slice-start
  345.8 4.5 slice-start.1
  345.8 4.5 slice-start.2
  350.3 72.1 %copy-start.19 = (f32[4,2]{0,1:T(2,128)S(1)}, f32[4,2]{0,1:T(2,128)}, u32[]{:S(2)}) copy-start(f32[4,2]{0,1:T(2,128)} %get-tuple-element.104) | copy-start | bytes 100
Sparse Core Ops, SparseCore 0:
  10.6 78.0 all-gather.9
  91.3 73.8 all-gather.11
  167.8 73.8 all-gather.13
  244.1 79.1 all-gather.17
  325.7 73.2 all-gather.15
  427.6 35.8 reduce-scatter.1
where the time goes:
time: 475 us; the launch traced here: 473 us
  waiting for transfers between devices  160 us (34%)
  blocking collectives  130 us (27%)
  other arithmetic  72 us (15%)
  local copies, waits for them, and re-layouts  62.6 us (13%)
  matrix products  31.2 us (7%)
  between operations  15.1 us (3%)
    all_gather x2, blocking collectives, merged(): pieces = jax.tree.map(lambda part: lax.all_gather(part, axis), value)  82.9 us
    all_gather x1, waiting for transfers between devices, per_device(): lax.all_gather(key_weight, 'dp', axis=0, tiled=True)  71 us
    all_gather x1, waiting for transfers between devices, per_device(): lax.all_gather(query_weight, 'dp', axis=0, tiled=True)  50.8 us
    all_gather x1, blocking collectives, per_device(): slot_queries = lax.all_gather(own_queries, 'dp', axis=0, tiled=True)  47.6 us
    reduce_scatter x1, waiting for transfers between devices, per_device(): lax.psum_scatter(terms.astype(jnp.bfloat16), 'fsdp', scatter_dimension=1,...  36 us
    add x31, other arithmetic, combine_pair(): rescale(early_mix, early_factor, HEAD)  30.6 us
    add x31, other arithmetic, combine_pair(): joined_total = early_total * early_factor + late_total * late_factor  21.6 us
    mul x62, local copies, waits for them, and re-layouts, rescale(): return (shaped * factor[:, :, None]).reshape(vectors.shape)  12.2 us
  transfers between devices with their start and end apart: 6, of which 3 were waited for; matrix products, arithmetic and copies ran while one was open for 34% of the time, Pallas kernels for 0%

commit v1 on v0

--- a/solution.py
+++ b/solution.py
@@ -151,7 +151,9 @@
         .astype(jnp.bfloat16)
     )
     own_queries = queries[group_rows:]
-    slot_queries = lax.all_gather(own_queries, "dp", axis=0, tiled=True)
+    slot_queries = jnp.concatenate(
+        lax.all_to_all(jnp.stack([own_queries] * lax.axis_size("dp")), "dp", 0, 0), axis=0
+    )
     pool_count = page_slots.shape[0]
     pool_local = pool_keys.shape[0]
     logical_of_slot = (

time: 475 us -> 449 us (0.945)
  blocking collectives: 130 us -> 83.1 us
  waiting for transfers between devices: 160 us -> 199 us
  other arithmetic: 72 us -> 49 us
  starting transfers between devices: 0.23 us -> 7.91 us
    all_gather x1 -> x0, blocking collectives: 47.6 us -> none  [per_device(): slot_queries = lax.all_gather(own_queries, 'dp', axis=0, tiled=True)]
    all_gather x1, waiting for transfers between devices: 0.01 us -> 22 us  [per_device(): lax.all_gather(value_weight, 'dp', axis=0, tiled=True)]
    add x31, other arithmetic: 21.6 us -> 0.78 us  [combine_pair(): joined_total = early_total * early_factor + late_total * late_factor]
    all_gather x1, waiting for transfers between devices: 50.8 us -> 58.9 us  [per_device(): lax.all_gather(query_weight, 'dp', axis=0, tiled=True)]
    all_to_all x0 -> x1, starting transfers between devices: none -> 7.49 us  [per_device(): lax.all_to_all(jnp.stack([own_queries] * lax.axis_size('dp')), 'dp', 0, 0)]
    all_gather x1, waiting for transfers between devices: 0.01 us -> 5.8 us  [per_device(): lax.all_gather(out_weight, 'dp', axis=1, tiled=True)]
  transfers between devices with their start and end apart: 6 -> 7, of which waited for: 3 -> 6; matrix products, arithmetic and copies ran while one was open for 34% -> 30% of each run, Pallas kernels for 0% -> 0%
where the time goes in v1:
time: 449 us; the launch traced here: 447 us
  waiting for transfers between devices  199 us (44%)
  blocking collectives  83.1 us (19%)
  local copies, waits for them, and re-layouts  60.7 us (14%)
  other arithmetic  49 us (11%)
  matrix products  31.3 us (7%)
  between operations  15.2 us (3%)
  starting transfers between devices  7.91 us (2%)
    all_gather x2, blocking collectives, merged(): pieces = jax.tree.map(lambda part: lax.all_gather(part, axis), value)  83.1 us
    all_gather x1, waiting for transfers between devices, per_device(): lax.all_gather(key_weight, 'dp', axis=0, tiled=True)  70.9 us
    all_gather x1, waiting for transfers between devices, per_device(): lax.all_gather(query_weight, 'dp', axis=0, tiled=True)  58.9 us
    reduce_scatter x1, waiting for transfers between devices, per_device(): lax.psum_scatter(terms.astype(jnp.bfloat16), 'fsdp', scatter_dimension=1,...  35.3 us
    add x31, other arithmetic, combine_pair(): rescale(early_mix, early_factor, HEAD)  30.6 us
    all_gather x1, waiting for transfers between devices, per_device(): lax.all_gather(value_weight, 'dp', axis=0, tiled=True)  22 us
    mul x62, local copies, waits for them, and re-layouts, rescale(): return (shaped * factor[:, :, None]).reshape(vectors.shape)  12.3 us
    dot_general x3, matrix products, per_device(): jnp.dot(normed, portion, preferred_element_type=jnp.float32)  9.45 us
  transfers between devices with their start and end apart: 7, of which 6 were waited for; matrix products, arithmetic and copies ran while one was open for 30% of the time, Pallas kernels for 0%

profile of v1, /device:TPU:8, one launch (start us, length us, event | category | flops | bytes accessed | tf_op | source)
XLA Modules:
  0.0 447.3 jit_solution(3134942566266047627)
XLA Ops:
  12.4 1.9 fusion.9
  14.7 6.2 %scatter_custom_fusion.1 = s32[1536]{0:T(1024)S(1)} fusion(s32[1536]{0:T(1024)S(1)} %compare_select_fusion, s32[1536]{0:T(1024)S(1)} %iota.55, s32[]{:T(128)} %constant.45.clone.1), kind=kCustom, calls=%fused_computation.111 | custom fusion | bytes 6148 | tf_op jit(solution)/shard_map/scatter | solution.py:162
  27.8 1.9 multiply_cosine_fusion
  29.8 58.9 %all-gather.9.cloned.1.call-done = bf16[2048,256]{1,0:T(8,128)(2,1)} async-done(((bf16[64,256]{1,0:T(8,128)(2,1)}), bf16[2048,256]{1,0:T(8,128)(2,1)}) %all-gather.9.cloned.1.call-update) | async-done | bytes 1048592 | tf_op jit(solution)/shard_map/all_gather | solution.py:89
  88.7 3.4 fusion.77
  92.1 2.1 reshape.289
  94.2 70.9 %all-gather.11.cloned.1.call-done = bf16[2048,256]{1,0:T(8,128)(2,1)} async-done(((bf16[64,256]{1,0:T(8,128)(2,1)}), bf16[2048,256]{1,0:T(8,128)(2,1)}) %all-gather.11.cloned.1.call-update) | async-done | bytes 1048592 | tf_op jit(solution)/shard_map/all_gather | solution.py:90
  165.2 3.4 fusion.78
  168.6 2.1 reshape.290
  170.7 2.7 fusion.74
  175.9 7.5 %all-to-all-start = ((bf16[32,4,256]{2,1,0:T(4,128)(2,1)}), bf16[32,4,256]{2,1,0:T(4,128)(2,1)S(1)}, u32[]{:S(2)}, u32[]{:S(2)}) async-start(bf16[32,4,256]{2,1,0:T(4,128)(2,1)} %stack.2), calls=%async_computation | async-start | bytes 131072 | tf_op jit(solution)/shard_map/all_to_all | solution.py:155
  183.6 4.7 %copy.102 = bf16[48,128,256]{1,2,0:T(8,128)(2,1)} copy(bf16[48,128,256]{2,1,0:T(8,128)(2,1)} %param.30) | data formatting | bytes 6291456 | tf_op jit(solution)/shard_map/reshape | solution.py:171
  188.4 3.8 all-to-all-done
  193.6 2.8 fusion.44
  199.8 2.5 fusion.13
  205.4 2.3 copy.100
  207.7 2.1 reshape_squeeze.6
  209.8 3.5 fusion.16
  214.9 1.9 fusion.4
  216.8 2.9 fusion.19
  219.7 22.0 %all-gather.13.cloned.1.call-done = bf16[2048,256]{1,0:T(8,128)(2,1)} async-done(((bf16[64,256]{1,0:T(8,128)(2,1)}), bf16[2048,256]{1,0:T(8,128)(2,1)}) %all-gather.13.cloned.1.call-update) | async-done | bytes 1048592 | tf_op jit(solution)/shard_map/all_gather | solution.py:91
  241.7 2.6 convolution_convert_fusion.1
  245.7 1.8 copy.101
  247.5 2.1 fusion.17
  249.6 3.2 fusion.24
  252.8 41.4 %all-gather = f32[4096,2]{0,1:T(2,128)S(1)} all-gather(f32[128,2]{0,1:T(2,128)S(1)} %select_reduce_fusion), channel_id=2, replica_groups=mesh['dp'=32,'fsdp'=8] {'dp'}, dimensions={0}, use_global_device_ids=true | all-gather | bytes 33792 | tf_op jit(solution)/shard_map/all_gather | solution.py:14
  294.4 41.7 %all-gather.1 = f32[4096,2]{0,1:T(2,128)S(1)} all-gather(f32[128,2]{0,1:T(2,128)S(1)} %fusion.50), channel_id=3, replica_groups=mesh['dp'=32,'fsdp'=8] {'dp'}, dimensions={0}, use_global_device_ids=true | all-gather | bytes 33792 | tf_op jit(solution)/shard_map/all_gather | solution.py:14
  336.2 4.5 %slice.113 = f32[3968,256]{1,0:T(8,128)} slice(f32[4096,256]{1,0:T(8,128)} %all-gather.17.cloned.1.call-done), slice={[128:4096], [0:256]} | slice | bytes 8126464 | tf_op jit(solution)/shard_map/slice | solution.py:16
  340.6 51.3 %while.14 = (s32[]{:T(128)}, f32[128,2]{0,1:T(2,128)S(1)}, f32[128,2]{0,1:T(2,128)S(1)}, f32[128,256]{1,0:T(8,128)S(1)}, f32[31,128,2]{1,2,0:T(2,128)S(1)}, /*in...) while((s32[]{:T(128)}, f32[128,2]{0,1:T(2,128)S(1)}, f32[128,2]{0,1:T(2,128)S(1)}, ...), condition=%wide.region_14.17_spmd, body=%wide.region_13.16_spmd.sunk | while | flops 99842 | bytes 931941 | solution.py:17
  393.3 5.8 %all-gather.15.cloned.1.call-done = bf16[256,2048]{0,1:T(8,128)(2,1)} async-done(((bf16[256,64]{0,1:T(8,128)(2,1)}), bf16[256,2048]{0,1:T(8,128)(2,1)}) %all-gather.15.cloned.1.call-update) | async-done | bytes 1048592 | tf_op jit(solution)/shard_map/all_gather | solution.py:222
  399.1 3.6 convolution_convert_fusion
  402.8 35.3 %reduce-scatter.2.cloned.1.call-done = bf16[516,256]{1,0:T(8,128)(2,1)} async-done(((bf16[516,2048]{1,0:T(8,128)(2,1)}), bf16[516,256]{1,0:T(8,128)(2,1)}) %reduce-scatter.2.cloned.1.call-update) | async-done | bytes 264208 | tf_op jit(solution)/shard_map/reduce_scatter | solution.py:225
  (320 shorter events, 79.9 us)
Async XLA Ops:
  7.2 192.6 %copy-start = (bf16[48,128,256]{2,1,0:T(8,128)(2,1)S(1)}, bf16[48,128,256]{2,1,0:T(8,128)(2,1)}, u32[]{:S(2)}) copy-start(bf16[48,128,256]{2,1,0:T(8,128)(2,1)} %param.31) | copy-start | bytes 9437188
  7.2 4.0 copy-start.14
  7.2 81.5 %all-gather.9.cloned.1.call-start = ((), (), s32[]{:S(2)}) async-start(), calls=%async_computation.2 | async-start | bytes 1081344 | tf_op jit(solution)/shard_map/all_gather | solution.py:89
  7.9 157.3 %all-gather.11.cloned.1.call-start = ((), (), s32[]{:S(2)}) async-start(), calls=%async_computation.3 | async-start | bytes 1081344 | tf_op jit(solution)/shard_map/all_gather | solution.py:90
  8.7 233.0 %all-gather.13.cloned.1.call-start = ((), (), s32[]{:S(2)}) async-start(), calls=%async_computation.4 | async-start | bytes 1081344 | tf_op jit(solution)/shard_map/all_gather | solution.py:91
  11.2 3.1 copy-start.2
  11.6 2.7 copy-start.20
  11.6 3.1 copy-start.15
  11.6 3.1 copy-start.21
  11.6 9.6 %copy-start.1 = (s32[128]{0:T(128)S(1)}, s32[128]{0:T(128)}, u32[]{:S(2)}) copy-start(s32[128]{0:T(128)} %param.35) | copy-start | bytes 1540
  27.1 156.5 %copy-start.17 = (s32[48]{0:T(128)}, s32[48]{0:T(128)S(1)}, u32[]{:S(2)}) copy-start(s32[48]{0:T(128)S(1)} %get-tuple-element.96) | copy-start | bytes 580
  29.8 166.7 %copy-start.13 = (pred[48,128]{1,0:T(8,128)(4,1)}, pred[48,128]{1,0:T(8,128)(4,1)S(1)}, u32[]{:S(2)}) copy-start(pred[48,128]{1,0:T(8,128)(4,1)S(1)} %add_compare_fusion) | copy-start | bytes 18436
  170.7 2.7 copy-start.8
  170.7 2.7 copy-start.9
  173.8 0.7 copy-start.4
  173.8 1.4 copy-start.6
  173.8 1.4 copy-start.7
  175.9 16.3 %all-to-all-start = ((bf16[32,4,256]{2,1,0:T(4,128)(2,1)}), bf16[32,4,256]{2,1,0:T(4,128)(2,1)S(1)}, u32[]{:S(2)}, u32[]{:S(2)}) async-start(bf16[32,4,256]{2,1,0:T(4,128)(2,1)} %stack.2), calls=%async_computation | async-start | bytes 131072 | tf_op jit(solution)/shard_map/all_to_all | solution.py:155
  183.4 152.8 %all-gather.17.cloned.1.call-start = ((), (), s32[]{:S(2)}) async-start(), calls=%async_computation.7 | async-start | bytes 4325376 | tf_op jit(solution)/shard_map/all_gather | solution.py:14
  188.4 8.1 %copy-start.16 = (s32[1024]{0:T(1024)}, s32[1024]{0:T(1024)S(1)}, u32[]{:S(2)}) copy-start(s32[1024]{0:T(1024)S(1)} %pad_clamp_fusion) | copy-start | bytes 12292
  204.0 195.1 %all-gather.15.cloned.1.call-start = ((), (), s32[]{:S(2)}) async-start(), calls=%async_computation.5 | async-start | bytes 1081344 | tf_op jit(solution)/shard_map/all_gather | solution.py:222
  204.6 233.5 %reduce-scatter.2.cloned.1.call-start = ((), (), s32[]{:S(2)}) async-start(), calls=%async_computation.6 | async-start | bytes 2396160 | tf_op jit(solution)/shard_map/reduce_scatter | solution.py:225
  209.8 3.5 copy-start.3
  209.8 3.5 copy-start.5
  214.9 1.9 copy-start.11
  219.6 27.8 %copy-start.10 = (pred[512,512]{0,1:T(8,128)(4,1)S(1)}, pred[512,512]{0,1:T(8,128)(4,1)}, u32[]{:S(2)}) copy-start(pred[512,512]{0,1:T(8,128)(4,1)} %iota_compare_fusion) | copy-start | bytes 786436
  244.3 0.7 copy-start.12
  249.6 44.6 %copy-start.18 = (s32[48]{0:T(128)S(1)}, s32[48]{0:T(128)}, u32[]{:S(2)}) copy-start(s32[48]{0:T(128)} %copy-done.17) | copy-start | bytes 580
  336.2 4.5 %slice-start = ((f32[4096,256]{1,0:T(8,128)}), f32[128,256]{1,0:T(8,128)S(1)}, s32[]{:S(2)}) async-start(f32[4096,256]{1,0:T(8,128)} %all-gather.17.cloned.1.call-done), calls=%async_computation.8 | async-start | bytes 262144 | tf_op jit(solution)/shard_map/slice | solution.py:15
  340.6 51.3 %copy-start.19 = (f32[4,2]{0,1:T(2,128)S(1)}, f32[4,2]{0,1:T(2,128)}, u32[]{:S(2)}) copy-start(f32[4,2]{0,1:T(2,128)} %get-tuple-element.97) | copy-start | bytes 100
Sparse Core Ops, SparseCore 0:
  10.6 78.0 all-gather.8
  91.3 73.8 all-gather.10
  167.8 73.8 all-gather.12
  244.1 79.1 all-gather.16
  325.7 73.3 all-gather.14
  402.9 35.1 reduce-scatter.1
